TPU v7x, 32 devices: a whole 2x2x4 slice. The times are simulated.
32 devices in a mesh: dp: 2 (over x), seq: 16 (over z, y, core).
Axes of the slice: x: 2, y: 2, z: 4, core: 2. Of those that a mesh axis runs over, the one named last changes fastest.
Arguments:
- frames: bfloat16 [2, 16, 64, 48, 128], P('dp', None, 'seq'), may hold values from -6 to 6
- frame_counts: int32 [2, 4], P('dp'), may hold values from 1 to 12, 16 in all within a row
- clip_group: int32 [2, 4], P('dp'), may hold values 0 or 1
- timesteps: int32 [2, 4], P('dp'), may hold values from 0 to 999
- owner_map: int32 [2, 16, 192, 1], P('dp', 'seq'), may hold values from 0 to 15; in each aligned block of 192 rows (0 to 191, 192 to 383, ..., all dimensions but the last counted through in order) at most 18 rows name the same one
- conv_weight: bfloat16 [3, 3, 3, 128, 128], replicated, may hold values from -0.109375 to 0.109375
- w_latent: bfloat16 [2048, 64], replicated, may hold values from -0.125 to 0.125
- hidden: bfloat16 [2, 4608, 3072], P('dp', 'seq'), may hold values from -6 to 6
- noise: float32 [2, 4608, 64], P('dp', 'seq'), may hold values from -6 to 6
- teacher: float32 [2, 4608, 64], P('dp', 'seq'), may hold values from -6 to 6
- w_out: bfloat16 [3072, 64], replicated, may hold values from -0.109375 to 0.109375
Outputs:
- latent: bfloat16 [2, 16, 16, 768], P('dp', None, 'seq')
- clip_loss: float32 [2, 4], P('dp')
- grad_out: float32 [3072, 64], P('seq')
Inputs may be any that keep to these rules, and one draw needn't show every extreme that they name: `owner_map`: among the tokens of one device no owner is named more than 18 times, a bound that some block reaches. `frame_counts`: the counts of a group sum to 16; the largest is exactly 12.
All inputs are finite; a program needn't handle non-finite values. No bound on the sum of `clip_group` on one device may be relied on, other than what follows from the above.
Results may differ from a plain program's by a relative error of at most 0.0055.
Values may be sent and summed in bfloat16 or wider, within the bound.
No kernel may reach another device: no remote copies, remote signals or barrier semaphores. Data moves between devices by JAX's collectives and lax.ppermute only.
A program may use at most 64 MiB of HBM per device.

v0:
```python
import jax
import jax.numpy as jnp
from jax import lax
from jax.sharding import PartitionSpec as P

LAT = 64
CLIPS = 4


def with_halo(cells, sides, width):
    for axis, dim in sides:
        count = lax.axis_size(axis)
        ends = count - 1
        head = lax.slice_in_dim(cells, 0, width, axis=dim)
        tail = lax.slice_in_dim(cells, cells.shape[dim] - width, cells.shape[dim], axis=dim)
        cells = jnp.concatenate(
            [
                lax.ppermute(tail, axis, [(i, (i + 1) % count) for i in range(ends)]),
                cells,
                lax.ppermute(head, axis, [((i + 1) % count, i) for i in range(ends)]),
            ],
            axis=dim,
        )
    return cells


def conv_rows(padded, kernel, keep, first, count):
    nframes = keep.shape[1]
    width = padded.shape[2] - 2
    chans = padded.shape[3]
    total = jnp.zeros((nframes, count * width, chans), jnp.float32)
    for lag in range(3):
        pieces = [
            padded[2 - lag : 2 - lag + nframes, first + i : first + i + count, j : j + width, :]
            for i in range(3)
            for j in range(3)
        ]
        columns = jnp.concatenate(pieces, axis=-1).reshape(-1, 9 * chans)
        part = jnp.dot(
            columns, kernel[lag].reshape(9 * chans, chans), preferred_element_type=jnp.float32
        )
        total = total + part.reshape(nframes, count * width, chans) * keep[lag][:, None, None]
    return total.reshape(nframes, count, width, chans)


def per_device(
    frames,
    frame_counts,
    clip_group,
    timesteps,
    owner_map,
    conv_weight,
    w_latent,
    hidden,
    noise,
    teacher,
    w_out,
):
    nseq = lax.axis_size("seq")
    local = frames[0]
    nframes, nrows, width, chans = local.shape
    tok_rows = nrows // 4
    tok_cols = width // 4
    per_frame = nrows * nseq // 4 * tok_cols
    counts = frame_counts[0]
    ends = jnp.cumsum(counts)
    index = jnp.arange(nframes, dtype=jnp.int32)
    clip_of = jnp.sum((index[:, None] >= ends[None, :]).astype(jnp.int32), axis=1)
    clip_hot = (clip_of[:, None] == jnp.arange(CLIPS, dtype=jnp.int32)[None, :]).astype(jnp.int32)
    starts = jnp.sum(clip_hot * (ends - counts)[None, :], axis=1)
    keep = jnp.stack([(index - lag >= starts).astype(jnp.float32) for lag in range(3)])
    rimmed = with_halo(frames, (("seq", 2),), 1)[0]
    outer_pad = jnp.pad(rimmed, ((2, 0), (0, 0), (1, 1), (0, 0)))
    conv = conv_rows(outer_pad, conv_weight, keep, 0, nrows)
    cells = (local.astype(jnp.float32) + jax.nn.silu(conv)).astype(jnp.bfloat16)
    patches = (
        cells.reshape(nframes, tok_rows, 4, tok_cols, 4, chans)
        .transpose(0, 1, 3, 2, 4, 5)
        .reshape(-1, 16 * chans)
    )
    tokens = jnp.dot(patches, w_latent, preferred_element_type=jnp.float32).astype(jnp.bfloat16)
    latent_out = tokens.reshape(1, nframes, tok_rows, tok_cols * LAT)
    slots = hidden.shape[1]
    capacity = slots // nseq
    owners = owner_map.reshape(-1)
    owner_hot = (owners[:, None] == jnp.arange(nseq, dtype=jnp.int32)[None, :]).astype(jnp.int32)
    rank = jnp.sum(jnp.cumsum(owner_hot, axis=0) * owner_hot, axis=1) - 1
    dest = owners * capacity + rank
    select = (dest[None, :] == jnp.arange(slots, dtype=jnp.int32)[:, None]).astype(jnp.bfloat16)
    tok_clip = jnp.repeat(clip_of, tok_rows * tok_cols).astype(jnp.float32) + 1.0
    outgoing = (
        jnp.dot(select, tokens, preferred_element_type=jnp.float32)
        .astype(jnp.bfloat16)
        .reshape(nseq, capacity, LAT)
    )
    labels = (
        jnp.dot(select, tok_clip.astype(jnp.bfloat16)[:, None], preferred_element_type=jnp.float32)
        .astype(jnp.bfloat16)
        .reshape(nseq, capacity)
    )
    arrived, arrived_tags = (
        lax.all_to_all(outgoing, "seq", split_axis=0, concat_axis=0, tiled=True),
        lax.all_to_all(labels, "seq", split_axis=0, concat_axis=0, tiled=True),
    )
    x0 = arrived.reshape(slots, LAT).astype(jnp.float32)
    tag = arrived_tags.reshape(slots).astype(jnp.float32)
    kind = clip_group[0].astype(jnp.float32)
    coef = (
        (2.0 * kind - 1.0)
        * (0.1 + timesteps[0].astype(jnp.float32) / 1000.0)
        / (counts.astype(jnp.float32) * per_frame)
    )
    slot_hot = (tag[:, None] == (jnp.arange(CLIPS, dtype=jnp.float32) + 1.0)[None, :]).astype(
        jnp.float32
    )
    slot_coef = jnp.sum(slot_hot * coef[None, :], axis=1)
    slot_kind = jnp.sum(slot_hot * kind[None, :], axis=1)
    states = hidden[0].astype(jnp.float32)
    mean = jnp.mean(states, axis=1, keepdims=True)
    centred = states - mean
    var = jnp.mean(centred * centred, axis=1, keepdims=True)
    normed = (centred * lax.rsqrt(var + 1e-06)).astype(jnp.bfloat16)
    pred = jnp.dot(normed, w_out, preferred_element_type=jnp.float32)
    target = slot_kind[:, None] * teacher[0] + (1.0 - slot_kind[:, None]) * (noise[0] - x0)
    diff = pred - target
    err = jnp.sum(diff * diff, axis=1)
    partial_loss = coef * jnp.sum(slot_hot * err[:, None], axis=0)
    clip_loss = lax.psum(partial_loss, "seq").reshape(1, CLIPS)
    dpred = (2.0 * slot_coef[:, None] * diff).astype(jnp.bfloat16)
    share_rows = normed.shape[1] // nseq
    grad_part = lax.dot_general(
        normed, dpred, (((0,), (0,)), ((), ())), preferred_element_type=jnp.float32
    )
    summed = lax.psum(grad_part, ("dp", "seq"))
    grad_mine = lax.dynamic_slice_in_dim(summed, lax.axis_index("seq") * share_rows, share_rows, 0)
    return (latent_out, clip_loss, grad_mine)


def solution(mesh):
    return jax.shard_map(
        per_device,
        mesh=mesh,
        in_specs=(
            P("dp", None, "seq", None, None),
            P("dp", None),
            P("dp", None),
            P("dp", None),
            P("dp", "seq", None, None),
            P(),
            P(),
            P("dp", "seq", None),
            P("dp", "seq", None),
            P("dp", "seq", None),
            P(),
        ),
        out_specs=(P("dp", None, "seq", None), P("dp", None), P("seq", None)),
        check_vma=False,
    )
```

profile of v0, /device:TPU:0, one launch (start us, length us, event | category | flops | bytes accessed | tf_op | source)
XLA Modules:
  0.0 210.9 jit_solution(1002889426171956777)
XLA Ops:
  7.2 2.0 fusion.43
  9.1 3.1 %collective-permute-start = (bf16[1,16,1,48,128]{4,3,2,1,0:T(8,128)(2,1)}, bf16[1,16,1,48,128]{4,3,2,1,0:T(8,128)(2,1)}, u32[]{:S(2)}, u32[]{:S(2)}) collective-permute-start(bf16[1,16,1,48,128]{4,3,2,1,0:T(8,128)(2,1)} %get-tuple-element.17), channel_id=1, source_target_pairs={{0,1},{1,2},{2,3},{3,4},{4,5},{5,6},{6,7},{7,8},{8,9},{9,10},{10,1... | collective-permute-start | bytes 589832 | tf_op jit(solution)/shard_map/ppermute | solution.py:18
  12.2 1.3 collective-permute-start.1
  13.5 0.8 reduce-window.10
  14.4 0.7 iota_compare_fusion.3
  15.1 0.6 reduce-window.11
  16.0 0.7 fusion.36
  16.7 0.7 add_add_fusion
  17.6 0.2 convolution_reduce_fusion
  17.8 0.7 all_to_all.12
  18.5 8.6 %all-to-all-start = ((bf16[16,1,18]{2,1,0:T(2,128)(2,1)}), bf16[16,1,18]{2,1,0:T(2,128)(2,1)S(1)}, u32[]{:S(2)}, u32[]{:S(2)}) async-start(bf16[16,1,18]{2,1,0:T(2,128)(2,1)} %all_to_all.12), calls=%async_computation | async-start | bytes 16384 | tf_op jit(solution)/shard_map/all_to_all | solution.py:103
  27.1 0.8 fusion.40
  27.9 1.9 fusion.42
  29.9 0.6 compare_convert_fusion.2
  30.5 1.2 convert_bitcast_fusion.2
  31.8 0.3 convert_reduce_fusion
  32.1 0.6 fusion.3
  32.7 0.7 fusion.4
  33.5 0.5 fusion.41
  34.0 0.6 iota_add_fusion
  34.6 1.6 copy.40
  36.3 0.8 fusion.37
  37.1 1.2 maximum_bitcast_fusion
  38.3 0.2 fusion.20
  38.5 0.2 fusion.21
  38.7 0.3 fusion.22
  39.0 0.3 fusion.23
  39.4 0.2 fusion.24
  39.6 0.3 fusion.25
  39.9 0.5 fusion.26
  40.4 0.5 fusion.27
  40.9 1.0 fusion.28
  41.9 0.3 fusion.7
  42.3 0.2 slice_dynamic-update-slice_fusion.1
  42.5 0.4 fusion.8
  42.9 0.4 fusion.9
  43.3 0.2 slice_dynamic-update-slice_fusion
  43.5 0.6 fusion.10
  44.1 0.4 fusion.13
  44.4 0.3 fusion.14
  44.8 0.2 fusion.15
  45.0 0.4 fusion.16
  45.4 0.3 fusion.17
  45.7 0.2 fusion.18
  45.9 0.4 fusion.19
  46.3 2.2 %fusion.45 = f32[16,192,128]{2,1,0:T(8,128)S(1)} fusion(bf16[16,192,1152]{2,1,0:T(8,128)(2,1)S(1)} %bitcast.85, bf16[1152,128,1]{1,0,2:T(8,128)(2,1)S(1)} %bitcast.90), kind=kOutput, calls=%fused_computation.117 | convolution fusion | flops 905969664 | bytes 8945664 | tf_op jit(solution)/shard_map/dot_general | solution.py:39
  48.6 2.0 fusion.44
  50.6 2.1 %multiply_add_fusion = f32[16,192,128]{2,1,0:T(8,128)S(1)} fusion(f32[16,192,128]{2,1,0:T(8,128)S(1)} %fusion.45, f32[16,192,128]{2,1,0:T(8,128)S(1)} %fusion.44, bf16[16,192,1152]{2,1,0:T(8,128)(2,1)S(1)} %bitcast.84, bf16[1152,128,1]{1,0,2:T(8,128)(2,1)S(1)} %bitcast.91, f32[16]{0:T(128)S(1)} %copy-done.10, f32[16]{0:T(128)S(1)} %copy-done.11, ...), kind=kOutput, calls=%fused_computation.8 | convolution fusion | flops 907935744 | bytes 12091584 | tf_op jit(solution)/shard_map/dot_general | solution.py:39
  52.8 0.9 copy.41
  53.7 0.5 copy-done.3
  54.2 0.4 fusion.29
  54.6 0.4 copy.42
  55.0 1.5 reshape.209
  56.5 1.5 convolution_convert_fusion.1
  58.0 0.2 convolution_convert_fusion
  58.4 0.7 reshape.236
  59.1 6.0 %all-to-all-start.1 = ((bf16[16,2,576]{2,1,0:T(2,128)(2,1)}), bf16[16,2,576]{2,1,0:T(2,128)(2,1)S(1)}, u32[]{:S(2)}, u32[]{:S(2)}) async-start(bf16[16,2,576]{2,1,0:T(2,128)(2,1)} %reshape.236), calls=%async_computation.1 | async-start | bytes 81920 | tf_op jit(solution)/shard_map/all_to_all | solution.py:102
  65.2 6.6 %all-to-all-done.1 = bf16[16,2,576]{2,1,0:T(2,128)(2,1)S(1)} async-done(((bf16[16,2,576]{2,1,0:T(2,128)(2,1)}), bf16[16,2,576]{2,1,0:T(2,128)(2,1)S(1)}, u32[]{:S(2)}, u32[]{:S(2)}) %all-to-all-start.1) | async-done | bytes 36896 | tf_op jit(solution)/shard_map/all_to_all | solution.py:102
  72.1 0.7 multiply_reduce_fusion
  73.1 1.4 fusion.34
  74.7 0.7 reshape.210
  75.4 30.2 %psum.14 = f32[1,4]{1,0:T(1,128)} all-reduce(f32[1,4]{1,0:T(1,128)S(1)} %multiply_bitcast_fusion), channel_id=1, replica_groups=mesh['dp'=2,'seq'=16] {'seq'}, use_global_device_ids=true, to_apply=%region_11.12 | all-reduce | flops 4 | bytes 32 | tf_op jit(solution)/shard_map/psum | solution.py:128
  105.5 96.9 %all-reduce.4.cloned.1.call-done = f32[3072,64]{0,1:T(8,128)} async-done(((f32[3072,64]{0,1:T(8,128)}), f32[3072,64]{0,1:T(8,128)}) %all-reduce.4.cloned.1.call-update) | async-done | bytes 786448 | tf_op jit(solution)/shard_map/psum | solution.py:134
  202.4 1.6 constant_dynamic-slice_fusion
  (66 shorter events, 1.7 us)
Async XLA Ops:
  7.2 64.9 %copy-start = (bf16[3072,64]{0,1:T(8,128)(2,1)S(1)}, bf16[3072,64]{0,1:T(8,128)(2,1)}, u32[]{:S(2)}) copy-start(bf16[3072,64]{0,1:T(8,128)(2,1)} %param.21) | copy-start | bytes 1179652
  7.2 24.6 %copy-start.1 = (bf16[1,288,3072]{2,1,0:T(8,128)(2,1)S(1)}, bf16[1,288,3072]{2,1,0:T(8,128)(2,1)}, u32[]{:S(2)}) copy-start(bf16[1,288,3072]{2,1,0:T(8,128)(2,1)} %param.18) | copy-start | bytes 5308420
  9.1 27.9 %collective-permute-start = (bf16[1,16,1,48,128]{4,3,2,1,0:T(8,128)(2,1)}, bf16[1,16,1,48,128]{4,3,2,1,0:T(8,128)(2,1)}, u32[]{:S(2)}, u32[]{:S(2)}) collective-permute-start(bf16[1,16,1,48,128]{4,3,2,1,0:T(8,128)(2,1)} %get-tuple-element.17), channel_id=1, source_target_pairs={{0,1},{1,2},{2,3},{3,4},{4,5},{5,6},{6,7},{7,8},{8,9},{9,10},{10,1... | collective-permute-start | bytes 589832 | tf_op jit(solution)/shard_map/ppermute | solution.py:18
  12.2 24.9 %collective-permute-start.1 = (bf16[1,16,1,48,128]{4,3,2,1,0:T(8,128)(2,1)}, bf16[1,16,1,48,128]{4,3,2,1,0:T(8,128)(2,1)}, u32[]{:S(2)}, u32[]{:S(2)}) collective-permute-start(bf16[1,16,1,48,128]{4,3,2,1,0:T(8,128)(2,1)} %get-tuple-element.18), channel_id=1, source_target_pairs={{1,0},{2,1},{3,2},{4,3},{5,4},{6,5},{7,6},{8,7},{9,8},{10,9},{11,1... | collective-permute-start | bytes 589832 | tf_op jit(solution)/shard_map/ppermute | solution.py:20
  17.4 1.1 copy-start.14
  18.5 17.7 %all-to-all-start = ((bf16[16,1,18]{2,1,0:T(2,128)(2,1)}), bf16[16,1,18]{2,1,0:T(2,128)(2,1)S(1)}, u32[]{:S(2)}, u32[]{:S(2)}) async-start(bf16[16,1,18]{2,1,0:T(2,128)(2,1)} %all_to_all.12), calls=%async_computation | async-start | bytes 16384 | tf_op jit(solution)/shard_map/all_to_all | solution.py:103
  27.1 5.6 %copy-start.2 = (bf16[1,288,3072]{2,1,0:T(8,128)(2,1)S(1)}, bf16[1,288,3072]{2,1,0:T(8,128)(2,1)}, u32[]{:S(2)}) copy-start(bf16[1,288,3072]{2,1,0:T(8,128)(2,1)} %param.18) | copy-start | bytes 5308420
  31.8 1.7 copy-start.16
  31.8 1.7 copy-start.17
  31.8 1.7 copy-start.18
  31.8 2.8 %copy-start.4 = (bf16[1,16,4,48,128]{4,3,2,1,0:T(8,128)(2,1)S(1)}, bf16[1,16,4,48,128]{4,3,2,1,0:T(8,128)(2,1)}, u32[]{:S(2)}) copy-start(bf16[1,16,4,48,128]{4,3,2,1,0:T(8,128)(2,1)} %param.11) | copy-start | bytes 2359300
  48.5 2.1 copy-start.5
  48.5 2.1 copy-start.9
  48.5 2.1 copy-start.10
  48.6 2.1 copy-start.11
  52.8 1.4 copy-start.3
  54.2 2.3 %copy-start.6 = (bf16[2048,64]{0,1:T(8,128)(2,1)S(1)}, bf16[2048,64]{0,1:T(8,128)(2,1)}, u32[]{:S(2)}) copy-start(bf16[2048,64]{0,1:T(8,128)(2,1)} %param.17) | copy-start | bytes 786436
  54.2 3.8 %copy-start.15 = (s32[192]{0:T(256)S(1)}, s32[192]{0:T(256)}, u32[]{:S(2)}) copy-start(s32[192]{0:T(256)} %copy-done.14) | copy-start | bytes 2308
  54.6 17.5 %copy-start.7 = (f32[1,288,64]{1,2,0:T(8,128)S(1)}, f32[1,288,64]{1,2,0:T(8,128)}, u32[]{:S(2)}) copy-start(f32[1,288,64]{1,2,0:T(8,128)} %param.19) | copy-start | bytes 221188
  54.6 17.5 %copy-start.8 = (f32[1,288,64]{1,2,0:T(8,128)S(1)}, f32[1,288,64]{1,2,0:T(8,128)}, u32[]{:S(2)}) copy-start(f32[1,288,64]{1,2,0:T(8,128)} %param.20) | copy-start | bytes 221188
  56.5 16.4 %copy-start.12 = (f32[4]{0:T(128)S(1)}, f32[4]{0:T(128)}, u32[]{:S(2)}) copy-start(f32[4]{0:T(128)} %iota_add_fusion) | copy-start | bytes 52
  56.5 16.4 %copy-start.13 = (f32[4]{0:T(128)S(1)}, f32[4]{0:T(128)}, u32[]{:S(2)}) copy-start(f32[4]{0:T(128)} %fusion.41) | copy-start | bytes 52
  59.1 12.7 %all-to-all-start.1 = ((bf16[16,2,576]{2,1,0:T(2,128)(2,1)}), bf16[16,2,576]{2,1,0:T(2,128)(2,1)S(1)}, u32[]{:S(2)}, u32[]{:S(2)}) async-start(bf16[16,2,576]{2,1,0:T(2,128)(2,1)} %reshape.236), calls=%async_computation.1 | async-start | bytes 81920 | tf_op jit(solution)/shard_map/all_to_all | solution.py:102
  65.1 137.3 %all-reduce.4.cloned.1.call-start = ((), (), s32[]{:S(2)}) async-start(), calls=%async_computation.2 | async-start | bytes 1572864 | tf_op jit(solution)/shard_map/psum | solution.py:134
Sparse Core Ops, SparseCore 0:
  74.7 127.7 all-reduce.3
where the time goes:
time: 211 us
  waiting for transfers between devices  104 us (49%)
  blocking collectives  30.2 us (14%)
  local copies, waits for them, and re-layouts  21.4 us (10%)
  starting transfers between devices  19 us (9%)
  between operations  14.6 us (7%)
  other arithmetic  11.7 us (6%)
  matrix products  10.4 us (5%)
    psum x1, waiting for transfers between devices, per_device(): summed = lax.psum(grad_part, ('dp', 'seq'))  96.9 us
    psum x1, blocking collectives, per_device(): clip_loss = lax.psum(partial_loss, 'seq').reshape(1, CLIPS)  30.2 us
    all_to_all x1, starting transfers between devices, per_device(): lax.all_to_all(labels, 'seq', split_axis=0, concat_axis=0, tiled=True)  8.62 us
    unnamed x59, local copies, waits for them, and re-layouts  7.35 us
    all_to_all x1, waiting for transfers between devices, per_device(): lax.all_to_all(outgoing, 'seq', split_axis=0, concat_axis=0, tiled=True)  6.64 us
    dot_general x3, matrix products, conv_rows(): jnp.dot(columns, kernel[lag].reshape(9 * chans, chans), preferred_element...  6.37 us
    all_to_all x1, starting transfers between devices, per_device(): lax.all_to_all(outgoing, 'seq', split_axis=0, concat_axis=0, tiled=True)  6.01 us
  transfers between devices with their start and end apart: 5, of which 2 were waited for; matrix products, arithmetic and copies ran while one was open for 7% of the time, Pallas kernels for 0%

commit v1 on v0

--- a/solution.py
+++ b/solution.py
@@ -5,6 +5,29 @@
 
 LAT = 64
 CLIPS = 4
+
+
+def cut_along(value, dim, size):
+    before, after = (value.shape[:dim], value.shape[dim + 1 :])
+    return jnp.moveaxis(value.reshape(*before, size, -1, *after), dim, 0)
+
+
+def joined_along(parts, dim):
+    parts = jnp.moveaxis(parts, 0, dim)
+    shape = parts.shape
+    return parts.reshape(*shape[:dim], shape[dim] * shape[dim + 1], *shape[dim + 2 :])
+
+
+def exchange_directly(x, axis, split_dim, concat_dim):
+    peers, index = (lax.axis_size(axis), lax.axis_index(axis))
+    blocks = cut_along(x, split_dim, peers)
+    result = blocks
+    for step in range(1, peers):
+        target, source = ((index + step) % peers, (index - step) % peers)
+        sent = lax.dynamic_index_in_dim(blocks, target, 0)
+        received = lax.ppermute(sent, axis, [(i, (i + step) % peers) for i in range(peers)])
+        result = lax.dynamic_update_slice_in_dim(result, received, source, axis=0)
+    return joined_along(result, concat_dim)
 
 
 def with_halo(cells, sides, width):
@@ -100,7 +123,7 @@
     )
     arrived, arrived_tags = (
         lax.all_to_all(outgoing, "seq", split_axis=0, concat_axis=0, tiled=True),
-        lax.all_to_all(labels, "seq", split_axis=0, concat_axis=0, tiled=True),
+        exchange_directly(labels, "seq", 0, 0),
     )
     x0 = arrived.reshape(slots, LAT).astype(jnp.float32)
     tag = arrived_tags.reshape(slots).astype(jnp.float32)

time: 211 us -> 239 us (1.13)
  starting transfers between devices: 19 us -> 36.3 us
  local copies, waits for them, and re-layouts: 21.4 us -> 32.4 us
    ppermute x0 -> x15, starting transfers between devices: none -> 26.8 us  [exchange_directly(): lax.ppermute(sent, axis, [(i, (i + step) % peers) for i in range(peers)])]
    dynamic_update_slice x0 -> x15, local copies, waits for them, and re-layouts: none -> 9.58 us  [exchange_directly(): result = lax.dynamic_update_slice_in_dim(result, received, source, axis=0)]
    all_to_all x1 -> x0, starting transfers between devices: 8.62 us -> none  [per_device(): lax.all_to_all(labels, 'seq', split_axis=0, concat_axis=0, tiled=True)]
    unnamed x59 -> x57, local copies, waits for them, and re-layouts: 7.35 us -> 7.35 us
  transfers between devices with their start and end apart: 5 -> 19, of which waited for: 2 -> 2; matrix products, arithmetic and copies ran while one was open for 7% -> 11% of each run, Pallas kernels for 0% -> 0%
where the time goes in v1:
time: 239 us
  waiting for transfers between devices  104 us (44%)
  starting transfers between devices  36.3 us (15%)
  local copies, waits for them, and re-layouts  32.4 us (14%)
  blocking collectives  30.2 us (13%)
  between operations  14.8 us (6%)
  other arithmetic  10.9 us (5%)
  matrix products  10.4 us (4%)
    psum x1, waiting for transfers between devices, per_device(): summed = lax.psum(grad_part, ('dp', 'seq'))  96.9 us
    psum x1, blocking collectives, per_device(): clip_loss = lax.psum(partial_loss, 'seq').reshape(1, CLIPS)  30.2 us
    ppermute x15, starting transfers between devices, exchange_directly(): lax.ppermute(sent, axis, [(i, (i + step) % peers) for i in range(peers)])  26.8 us
    dynamic_update_slice x15, local copies, waits for them, and re-layouts, exchange_directly(): result = lax.dynamic_update_slice_in_dim(result, received, source, axis=0)  9.58 us
    unnamed x57, local copies, waits for them, and re-layouts  7.35 us
    all_to_all x1, waiting for transfers between devices, per_device(): lax.all_to_all(outgoing, 'seq', split_axis=0, concat_axis=0, tiled=True)  6.64 us
    dot_general x3, matrix products, conv_rows(): jnp.dot(columns, kernel[lag].reshape(9 * chans, chans), preferred_element...  6.34 us
    all_to_all x1, starting transfers between devices, per_device(): lax.all_to_all(outgoing, 'seq', split_axis=0, concat_axis=0, tiled=True)  5.18 us
  transfers between devices with their start and end apart: 19, of which 2 were waited for; matrix products, arithmetic and copies ran while one was open for 11% of the time, Pallas kernels for 0%

profile of v1, /device:TPU:0, one launch (start us, length us, event | category | flops | bytes accessed | tf_op | source)
XLA Modules:
  0.0 238.6 jit_solution(17347664633009379350)
XLA Ops:
  7.2 2.0 fusion.43
  9.2 3.1 %collective-permute-start = (bf16[1,16,1,48,128]{4,3,2,1,0:T(8,128)(2,1)}, bf16[1,16,1,48,128]{4,3,2,1,0:T(8,128)(2,1)}, u32[]{:S(2)}, u32[]{:S(2)}) collective-permute-start(bf16[1,16,1,48,128]{4,3,2,1,0:T(8,128)(2,1)} %get-tuple-element.17), channel_id=1, source_target_pairs={{0,1},{1,2},{2,3},{3,4},{4,5},{5,6},{6,7},{7,8},{8,9},{9,10},{10,1... | collective-permute-start | bytes 589832 | tf_op jit(solution)/shard_map/ppermute | solution.py:41
  12.2 1.3 collective-permute-start.1
  13.7 0.8 reduce-window.10
  14.6 0.7 iota_compare_fusion.3
  15.3 0.6 reduce-window.11
  16.2 0.7 fusion.36
  16.9 0.7 add_add_fusion
  18.2 0.7 constant_dynamic-slice_fusion.1
  18.9 2.6 %collective-permute-start.2 = (bf16[1,1,18]{2,0,1:T(2,128)(2,1)}, bf16[1,1,18]{2,0,1:T(2,128)(2,1)}, u32[]{:S(2)}, u32[]{:S(2)}) collective-permute-start(bf16[1,1,18]{2,0,1:T(2,128)(2,1)} %get-tuple-element.33), channel_id=1, source_target_pairs={{0,1},{1,2},{2,3},{3,4},{4,5},{5,6},{6,7},{7,8},{8,9},{9,10},{10,1... | collective-permute-start | bytes 116 | tf_op jit(solution)/shard_map/ppermute | solution.py:28
  21.5 1.7 collective-permute-start.3
  23.2 2.4 %collective-permute-start.4 = (bf16[1,1,18]{2,0,1:T(2,128)(2,1)}, bf16[1,1,18]{2,0,1:T(2,128)(2,1)}, u32[]{:S(2)}, u32[]{:S(2)}) collective-permute-start(bf16[1,1,18]{2,0,1:T(2,128)(2,1)} %get-tuple-element.31), channel_id=1, source_target_pairs={{0,3},{1,4},{2,5},{3,6},{4,7},{5,8},{6,9},{7,10},{8,11},{9,12},{10... | collective-permute-start | bytes 116 | tf_op jit(solution)/shard_map/ppermute | solution.py:28
  25.6 0.7 fusion.40
  26.3 2.8 %copy.30 = f32[1,16,4,48,128]{4,1,3,2,0:T(8,128)} copy(bf16[1,16,4,48,128]{4,3,2,1,0:T(8,128)(2,1)} %param.11) | data formatting | bytes 2359296 | tf_op jit(solution)/shard_map/convert_element_type | solution.py:98
  29.0 2.1 fusion.42
  31.2 0.5 compare_convert_fusion.2
  31.7 0.5 convert_bitcast_fusion.2
  32.6 0.6 fusion.3
  33.2 0.7 fusion.4
  33.9 0.6 fusion.41
  34.5 0.6 iota_add_fusion
  35.1 1.6 collective-permute-start.5
  36.7 0.6 dynamic_update_slice.45
  37.3 0.7 collective-permute-start.6
  38.1 0.6 dynamic_update_slice.46
  38.7 1.6 collective-permute-start.7
  40.3 0.6 dynamic_update_slice.47
  40.9 4.4 %collective-permute-start.8 = (bf16[1,1,18]{2,0,1:T(2,128)(2,1)}, bf16[1,1,18]{2,0,1:T(2,128)(2,1)}, u32[]{:S(2)}, u32[]{:S(2)}) collective-permute-start(bf16[1,1,18]{2,0,1:T(2,128)(2,1)} %get-tuple-element.27), channel_id=1, source_target_pairs={{0,7},{1,8},{2,9},{3,10},{4,11},{5,12},{6,13},{7,14},{8,15},{9,0},... | collective-permute-start | bytes 116 | tf_op jit(solution)/shard_map/ppermute | solution.py:28
  45.3 0.6 dynamic_update_slice.48
  46.3 0.6 dynamic_update_slice.49
  47.3 0.7 dynamic_update_slice.50
  48.0 2.1 collective-permute-start.11
  50.0 0.6 dynamic_update_slice.51
  50.7 2.4 %collective-permute-start.12 = (bf16[1,1,18]{2,0,1:T(2,128)(2,1)}, bf16[1,1,18]{2,0,1:T(2,128)(2,1)}, u32[]{:S(2)}, u32[]{:S(2)}) collective-permute-start(bf16[1,1,18]{2,0,1:T(2,128)(2,1)} %get-tuple-element.23), channel_id=1, source_target_pairs={{0,11},{1,12},{2,13},{3,14},{4,15},{5,0},{6,1},{7,2},{8,3},{9,4},{... | collective-permute-start | bytes 116 | tf_op jit(solution)/shard_map/ppermute | solution.py:28
  53.1 0.7 dynamic_update_slice.52
  53.8 1.9 collective-permute-start.13
  55.7 0.6 dynamic_update_slice.53
  56.4 0.6 dynamic_update_slice.54
  57.0 2.2 collective-permute-start.15
  59.2 0.6 dynamic_update_slice.55
  59.8 2.3 collective-permute-start.16
  62.1 0.7 dynamic_update_slice.56
  62.8 0.6 dynamic_update_slice.57
  63.4 0.7 dynamic_update_slice.58
  64.1 0.7 dynamic_update_slice.59
  64.9 0.8 fusion.37
  65.7 1.2 maximum_bitcast_fusion
  69.5 1.0 fusion.28
  72.1 0.6 fusion.10
  74.9 2.0 fusion.45
  76.9 2.3 fusion.44
  79.2 2.1 multiply_add_fusion
  81.3 0.9 copy.31
  83.5 1.5 reshape.203
  85.0 1.5 convolution_convert_fusion.1
  86.9 0.7 reshape.223
  87.7 5.2 %all-to-all-start = ((bf16[16,2,576]{2,1,0:T(2,128)(2,1)}), bf16[16,2,576]{2,1,0:T(2,128)(2,1)S(1)}, u32[]{:S(2)}, u32[]{:S(2)}) async-start(bf16[16,2,576]{2,1,0:T(2,128)(2,1)} %reshape.223), calls=%async_computation | async-start | bytes 81920 | tf_op jit(solution)/shard_map/all_to_all | solution.py:125
  92.9 6.6 %all-to-all-done = bf16[16,2,576]{2,1,0:T(2,128)(2,1)S(1)} async-done(((bf16[16,2,576]{2,1,0:T(2,128)(2,1)}), bf16[16,2,576]{2,1,0:T(2,128)(2,1)S(1)}, u32[]{:S(2)}, u32[]{:S(2)}) %all-to-all-start) | async-done | bytes 36896 | tf_op jit(solution)/shard_map/all_to_all | solution.py:125
  99.9 0.7 multiply_reduce_fusion
  100.8 1.4 fusion.34
  102.4 0.7 reshape.204
  103.1 30.2 %psum.14 = f32[1,4]{1,0:T(1,128)} all-reduce(f32[1,4]{1,0:T(1,128)S(1)} %multiply_bitcast_fusion), channel_id=1, replica_groups=mesh['dp'=2,'seq'=16] {'seq'}, use_global_device_ids=true, to_apply=%region_11.12 | all-reduce | flops 4 | bytes 32 | tf_op jit(solution)/shard_map/psum | solution.py:151
  133.3 96.9 %all-reduce.4.cloned.1.call-done = f32[3072,64]{0,1:T(8,128)} async-done(((f32[3072,64]{0,1:T(8,128)}), f32[3072,64]{0,1:T(8,128)}) %all-reduce.4.cloned.1.call-update) | async-done | bytes 786448 | tf_op jit(solution)/shard_map/psum | solution.py:157
  230.2 1.6 constant_dynamic-slice_fusion
  (107 shorter events, 10.8 us)
Async XLA Ops:
  7.2 92.7 %copy-start = (bf16[3072,64]{0,1:T(8,128)(2,1)S(1)}, bf16[3072,64]{0,1:T(8,128)(2,1)}, u32[]{:S(2)}) copy-start(bf16[3072,64]{0,1:T(8,128)(2,1)} %param.21) | copy-start | bytes 1179652
  7.2 24.5 %copy-start.16 = (s32[1,4]{1,0:T(1,128)S(1)}, s32[1,4]{1,0:T(1,128)}, u32[]{:S(2)}) copy-start(s32[1,4]{1,0:T(1,128)} %param.13) | copy-start | bytes 52
  7.2 25.0 %copy-start.1 = (bf16[1,288,3072]{2,1,0:T(8,128)(2,1)S(1)}, bf16[1,288,3072]{2,1,0:T(8,128)(2,1)}, u32[]{:S(2)}) copy-start(bf16[1,288,3072]{2,1,0:T(8,128)(2,1)} %param.18) | copy-start | bytes 5308420
  9.2 56.5 %collective-permute-start = (bf16[1,16,1,48,128]{4,3,2,1,0:T(8,128)(2,1)}, bf16[1,16,1,48,128]{4,3,2,1,0:T(8,128)(2,1)}, u32[]{:S(2)}, u32[]{:S(2)}) collective-permute-start(bf16[1,16,1,48,128]{4,3,2,1,0:T(8,128)(2,1)} %get-tuple-element.17), channel_id=1, source_target_pairs={{0,1},{1,2},{2,3},{3,4},{4,5},{5,6},{6,7},{7,8},{8,9},{9,10},{10,1... | collective-permute-start | bytes 589832 | tf_op jit(solution)/shard_map/ppermute | solution.py:41
  12.2 53.4 %collective-permute-start.1 = (bf16[1,16,1,48,128]{4,3,2,1,0:T(8,128)(2,1)}, bf16[1,16,1,48,128]{4,3,2,1,0:T(8,128)(2,1)}, u32[]{:S(2)}, u32[]{:S(2)}) collective-permute-start(bf16[1,16,1,48,128]{4,3,2,1,0:T(8,128)(2,1)} %get-tuple-element.18), channel_id=1, source_target_pairs={{1,0},{2,1},{3,2},{4,3},{5,4},{6,5},{7,6},{8,7},{9,8},{10,9},{11,1... | collective-permute-start | bytes 589832 | tf_op jit(solution)/shard_map/ppermute | solution.py:43
  17.6 13.5 %copy-start.12 = (s32[192]{0:T(256)}, s32[192]{0:T(256)S(1)}, u32[]{:S(2)}) copy-start(s32[192]{0:T(256)S(1)} %add_add_fusion) | copy-start | bytes 2308
  18.9 16.3 %collective-permute-start.2 = (bf16[1,1,18]{2,0,1:T(2,128)(2,1)}, bf16[1,1,18]{2,0,1:T(2,128)(2,1)}, u32[]{:S(2)}, u32[]{:S(2)}) collective-permute-start(bf16[1,1,18]{2,0,1:T(2,128)(2,1)} %get-tuple-element.33), channel_id=1, source_target_pairs={{0,1},{1,2},{2,3},{3,4},{4,5},{5,6},{6,7},{7,8},{8,9},{9,10},{10,1... | collective-permute-start | bytes 116 | tf_op jit(solution)/shard_map/ppermute | solution.py:28
  21.5 15.8 %collective-permute-start.3 = (bf16[1,1,18]{2,0,1:T(2,128)(2,1)}, bf16[1,1,18]{2,0,1:T(2,128)(2,1)}, u32[]{:S(2)}, u32[]{:S(2)}) collective-permute-start(bf16[1,1,18]{2,0,1:T(2,128)(2,1)} %get-tuple-element.32), channel_id=1, source_target_pairs={{0,2},{1,3},{2,4},{3,5},{4,6},{5,7},{6,8},{7,9},{8,10},{9,11},{10,... | collective-permute-start | bytes 116 | tf_op jit(solution)/shard_map/ppermute | solution.py:28
  23.2 15.5 %collective-permute-start.4 = (bf16[1,1,18]{2,0,1:T(2,128)(2,1)}, bf16[1,1,18]{2,0,1:T(2,128)(2,1)}, u32[]{:S(2)}, u32[]{:S(2)}) collective-permute-start(bf16[1,1,18]{2,0,1:T(2,128)(2,1)} %get-tuple-element.31), channel_id=1, source_target_pairs={{0,3},{1,4},{2,5},{3,6},{4,7},{5,8},{6,9},{7,10},{8,11},{9,12},{10... | collective-permute-start | bytes 116 | tf_op jit(solution)/shard_map/ppermute | solution.py:28
  29.0 4.2 %copy-start.2 = (bf16[1,288,3072]{2,1,0:T(8,128)(2,1)S(1)}, bf16[1,288,3072]{2,1,0:T(8,128)(2,1)}, u32[]{:S(2)}) copy-start(bf16[1,288,3072]{2,1,0:T(8,128)(2,1)} %param.18) | copy-start | bytes 5308420
  32.2 1.7 copy-start.14
  32.2 1.7 copy-start.15
  32.2 1.7 copy-start.17
  32.2 33.4 %copy-start.4 = (bf16[1,16,4,48,128]{4,3,2,1,0:T(8,128)(2,1)S(1)}, bf16[1,16,4,48,128]{4,3,2,1,0:T(8,128)(2,1)}, u32[]{:S(2)}) copy-start(bf16[1,16,4,48,128]{4,3,2,1,0:T(8,128)(2,1)} %param.11) | copy-start | bytes 2359300
  35.1 5.8 %collective-permute-start.5 = (bf16[1,1,18]{2,0,1:T(2,128)(2,1)}, bf16[1,1,18]{2,0,1:T(2,128)(2,1)}, u32[]{:S(2)}, u32[]{:S(2)}) collective-permute-start(bf16[1,1,18]{2,0,1:T(2,128)(2,1)} %get-tuple-element.30), channel_id=1, source_target_pairs={{0,4},{1,5},{2,6},{3,7},{4,8},{5,9},{6,10},{7,11},{8,12},{9,13},{1... | collective-permute-start | bytes 116 | tf_op jit(solution)/shard_map/ppermute | solution.py:28
  37.3 8.6 %collective-permute-start.6 = (bf16[1,1,18]{2,0,1:T(2,128)(2,1)}, bf16[1,1,18]{2,0,1:T(2,128)(2,1)}, u32[]{:S(2)}, u32[]{:S(2)}) collective-permute-start(bf16[1,1,18]{2,0,1:T(2,128)(2,1)} %get-tuple-element.29), channel_id=1, source_target_pairs={{0,5},{1,6},{2,7},{3,8},{4,9},{5,10},{6,11},{7,12},{8,13},{9,14},{... | collective-permute-start | bytes 116 | tf_op jit(solution)/shard_map/ppermute | solution.py:28
  38.7 8.3 %collective-permute-start.7 = (bf16[1,1,18]{2,0,1:T(2,128)(2,1)}, bf16[1,1,18]{2,0,1:T(2,128)(2,1)}, u32[]{:S(2)}, u32[]{:S(2)}) collective-permute-start(bf16[1,1,18]{2,0,1:T(2,128)(2,1)} %get-tuple-element.28), channel_id=1, source_target_pairs={{0,6},{1,7},{2,8},{3,9},{4,10},{5,11},{6,12},{7,13},{8,14},{9,15},... | collective-permute-start | bytes 116 | tf_op jit(solution)/shard_map/ppermute | solution.py:28
  40.9 7.0 %collective-permute-start.8 = (bf16[1,1,18]{2,0,1:T(2,128)(2,1)}, bf16[1,1,18]{2,0,1:T(2,128)(2,1)}, u32[]{:S(2)}, u32[]{:S(2)}) collective-permute-start(bf16[1,1,18]{2,0,1:T(2,128)(2,1)} %get-tuple-element.27), channel_id=1, source_target_pairs={{0,7},{1,8},{2,9},{3,10},{4,11},{5,12},{6,13},{7,14},{8,15},{9,0},... | collective-permute-start | bytes 116 | tf_op jit(solution)/shard_map/ppermute | solution.py:28
  45.9 4.7 %collective-permute-start.9 = (bf16[1,1,18]{2,0,1:T(2,128)(2,1)}, bf16[1,1,18]{2,0,1:T(2,128)(2,1)}, u32[]{:S(2)}, u32[]{:S(2)}) collective-permute-start(bf16[1,1,18]{2,0,1:T(2,128)(2,1)} %get-tuple-element.26), channel_id=1, source_target_pairs={{0,8},{1,9},{2,10},{3,11},{4,12},{5,13},{6,14},{7,15},{8,0},{9,1},... | collective-permute-start | bytes 116 | tf_op jit(solution)/shard_map/ppermute | solution.py:28
  46.9 6.8 %collective-permute-start.10 = (bf16[1,1,18]{2,0,1:T(2,128)(2,1)}, bf16[1,1,18]{2,0,1:T(2,128)(2,1)}, u32[]{:S(2)}, u32[]{:S(2)}) collective-permute-start(bf16[1,1,18]{2,0,1:T(2,128)(2,1)} %get-tuple-element.25), channel_id=1, source_target_pairs={{0,9},{1,10},{2,11},{3,12},{4,13},{5,14},{6,15},{7,0},{8,1},{9,2},... | collective-permute-start | bytes 116 | tf_op jit(solution)/shard_map/ppermute | solution.py:28
  48.0 8.4 %collective-permute-start.11 = (bf16[1,1,18]{2,0,1:T(2,128)(2,1)}, bf16[1,1,18]{2,0,1:T(2,128)(2,1)}, u32[]{:S(2)}, u32[]{:S(2)}) collective-permute-start(bf16[1,1,18]{2,0,1:T(2,128)(2,1)} %get-tuple-element.24), channel_id=1, source_target_pairs={{0,10},{1,11},{2,12},{3,13},{4,14},{5,15},{6,0},{7,1},{8,2},{9,3},... | collective-permute-start | bytes 116 | tf_op jit(solution)/shard_map/ppermute | solution.py:28
  50.7 6.3 %collective-permute-start.12 = (bf16[1,1,18]{2,0,1:T(2,128)(2,1)}, bf16[1,1,18]{2,0,1:T(2,128)(2,1)}, u32[]{:S(2)}, u32[]{:S(2)}) collective-permute-start(bf16[1,1,18]{2,0,1:T(2,128)(2,1)} %get-tuple-element.23), channel_id=1, source_target_pairs={{0,11},{1,12},{2,13},{3,14},{4,15},{5,0},{6,1},{7,2},{8,3},{9,4},{... | collective-permute-start | bytes 116 | tf_op jit(solution)/shard_map/ppermute | solution.py:28
  53.8 6.1 %collective-permute-start.13 = (bf16[1,1,18]{2,0,1:T(2,128)(2,1)}, bf16[1,1,18]{2,0,1:T(2,128)(2,1)}, u32[]{:S(2)}, u32[]{:S(2)}) collective-permute-start(bf16[1,1,18]{2,0,1:T(2,128)(2,1)} %get-tuple-element.22), channel_id=1, source_target_pairs={{0,12},{1,13},{2,14},{3,15},{4,0},{5,1},{6,2},{7,3},{8,4},{9,5},{1... | collective-permute-start | bytes 116 | tf_op jit(solution)/shard_map/ppermute | solution.py:28
  56.3 6.4 %collective-permute-start.14 = (bf16[1,1,18]{2,0,1:T(2,128)(2,1)}, bf16[1,1,18]{2,0,1:T(2,128)(2,1)}, u32[]{:S(2)}, u32[]{:S(2)}) collective-permute-start(bf16[1,1,18]{2,0,1:T(2,128)(2,1)} %get-tuple-element.21), channel_id=1, source_target_pairs={{0,13},{1,14},{2,15},{3,0},{4,1},{5,2},{6,3},{7,4},{8,5},{9,6},{10... | collective-permute-start | bytes 116 | tf_op jit(solution)/shard_map/ppermute | solution.py:28
  57.0 6.4 %collective-permute-start.15 = (bf16[1,1,18]{2,0,1:T(2,128)(2,1)}, bf16[1,1,18]{2,0,1:T(2,128)(2,1)}, u32[]{:S(2)}, u32[]{:S(2)}) collective-permute-start(bf16[1,1,18]{2,0,1:T(2,128)(2,1)} %get-tuple-element.20), channel_id=1, source_target_pairs={{0,14},{1,15},{2,0},{3,1},{4,2},{5,3},{6,4},{7,5},{8,6},{9,7},{10,... | collective-permute-start | bytes 116 | tf_op jit(solution)/shard_map/ppermute | solution.py:28
  59.8 4.3 %collective-permute-start.16 = (bf16[1,1,18]{2,0,1:T(2,128)(2,1)S(1)}, bf16[1,1,18]{2,0,1:T(2,128)(2,1)}, u32[]{:S(2)}, u32[]{:S(2)}) collective-permute-start(bf16[1,1,18]{2,0,1:T(2,128)(2,1)S(1)} %get-tuple-element.19), channel_id=1, source_target_pairs={{0,15},{1,0},{2,1},{3,2},{4,3},{5,4},{6,5},{7,6},{8,7},{9,8},{10,9... | collective-permute-start | bytes 116 | tf_op jit(solution)/shard_map/ppermute | solution.py:28
  76.9 2.3 copy-start.5
  76.9 2.3 copy-start.9
  81.3 1.4 copy-start.3
  82.7 2.3 copy-start.6
  82.7 3.9 %copy-start.13 = (s32[192]{0:T(256)S(1)}, s32[192]{0:T(256)}, u32[]{:S(2)}) copy-start(s32[192]{0:T(256)} %copy-done.12) | copy-start | bytes 2308
  83.1 16.7 %copy-start.7 = (f32[1,288,64]{1,2,0:T(8,128)S(1)}, f32[1,288,64]{1,2,0:T(8,128)}, u32[]{:S(2)}) copy-start(f32[1,288,64]{1,2,0:T(8,128)} %param.19) | copy-start | bytes 221188
  83.1 16.7 %copy-start.8 = (f32[1,288,64]{1,2,0:T(8,128)S(1)}, f32[1,288,64]{1,2,0:T(8,128)}, u32[]{:S(2)}) copy-start(f32[1,288,64]{1,2,0:T(8,128)} %param.20) | copy-start | bytes 221188
  85.0 15.6 %copy-start.10 = (f32[4]{0:T(128)S(1)}, f32[4]{0:T(128)}, u32[]{:S(2)}) copy-start(f32[4]{0:T(128)} %iota_add_fusion) | copy-start | bytes 52
  85.0 15.6 %copy-start.11 = (f32[4]{0:T(128)S(1)}, f32[4]{0:T(128)}, u32[]{:S(2)}) copy-start(f32[4]{0:T(128)} %fusion.41) | copy-start | bytes 52
  87.7 11.9 %all-to-all-start = ((bf16[16,2,576]{2,1,0:T(2,128)(2,1)}), bf16[16,2,576]{2,1,0:T(2,128)(2,1)S(1)}, u32[]{:S(2)}, u32[]{:S(2)}) async-start(bf16[16,2,576]{2,1,0:T(2,128)(2,1)} %reshape.223), calls=%async_computation | async-start | bytes 81920 | tf_op jit(solution)/shard_map/all_to_all | solution.py:125
  92.9 137.3 %all-reduce.4.cloned.1.call-start = ((), (), s32[]{:S(2)}) async-start(), calls=%async_computation.1 | async-start | bytes 1572864 | tf_op jit(solution)/shard_map/psum | solution.py:157
Sparse Core Ops, SparseCore 0:
  102.4 127.7 all-reduce.3
